TPU v7x, 128 devices: a whole 4x4x4 slice. The times are simulated.
128 devices in a mesh: rep: 4 (over x), fsdp: 2 (over core), tp: 16 (over z, y).
Axes of the slice: x: 4, y: 4, z: 4, core: 2. Of those that a mesh axis runs over, the one named last changes fastest.
Arguments:
- tokens: bfloat16 [8192, 2048], P(('rep', 'fsdp'), 'tp'), may hold values from -6 to 6
- cotangent: bfloat16 [8192, 2048], P(('rep', 'fsdp'), 'tp'), may hold values from -6 to 6
- frame_mask: int32 [8192], P(('rep', 'fsdp')), may hold values 0 or 1
- ln_gain: bfloat16 [2048], P('tp'), may hold values from 0.099609375 to 1.8984375
- ln_bias: bfloat16 [2048], P('tp'), may hold values from -3 to 3
- weight_in: bfloat16 [2048, 8192], P('fsdp', 'tp'), may hold values from -0.1875 to 0.1875
- weight_out: bfloat16 [8192, 2048], P('tp', 'fsdp'), may hold values from -0.09375 to 0.09375
- blocks_in: int32 [16, 64], P('fsdp', 'tp'), may hold values 0 or 1
- blocks_out: int32 [64, 16], P('tp', 'fsdp'), may hold values 0 or 1
Outputs:
- block_out: bfloat16 [8192, 2048], P(('rep', 'fsdp'), 'tp')
- input_grad: bfloat16 [8192, 2048], P(('rep', 'fsdp'), 'tp')
- grad_in: float32 [2048, 8192], P('fsdp', 'tp')
- grad_out: float32 [8192, 2048], P('tp', 'fsdp')
- grad_gain: float32 [2048], P('tp')
- grad_bias: float32 [2048], P('tp')
All inputs are finite; a program needn't handle non-finite values. No bound on the sum of `frame_mask` or of `blocks_in` or of `blocks_out` on one device may be relied on, other than what follows from the above.
Results may differ from a plain program's by a relative error of at most 0.019.
Values may be sent and summed in bfloat16 or wider, within the bound.
No kernel may reach another device: no remote copies, remote signals or barrier semaphores. Data moves between devices by JAX's collectives and lax.ppermute only.
A program may use at most 128 MiB of HBM per device.

v0:
```python
from functools import partial
import jax
import jax.numpy as jnp
from jax import lax
from jax.sharding import PartitionSpec as P

BLK = 128


def apply_blocks(weight, blocks, kind):
    row_blocks, col_blocks = blocks.shape
    shaped = weight.reshape(row_blocks, BLK, col_blocks, BLK)
    keeper = blocks.astype(kind)[:, None, :, None]
    return (shaped * keeper).reshape(weight.shape)


def contract_rows(left, right):
    return lax.dot_general(
        left, right, (((0,), (0,)), ((), ())), preferred_element_type=jnp.float32
    )


def contract_cols(left, right):
    return lax.dot_general(
        left, right, (((1,), (1,)), ((), ())), preferred_element_type=jnp.float32
    )


def on_device(
    tokens, cotangent, frame_mask, ln_gain, ln_bias, weight_in, weight_out, blocks_in, blocks_out
):
    whole_rows, whole_grad, gain_full, bias_full = (
        lax.all_gather(tokens, "tp", axis=1, tiled=True),
        lax.all_gather(cotangent, "tp", axis=1, tiled=True),
        lax.all_gather(ln_gain, "tp", axis=0, tiled=True),
        lax.all_gather(ln_bias, "tp", axis=0, tiled=True),
    )
    masked_in = apply_blocks(weight_in, blocks_in, jnp.bfloat16)
    masked_out = apply_blocks(weight_out, blocks_out, jnp.bfloat16)
    full_in, full_out = (
        lax.all_gather(masked_in, "fsdp", axis=0, tiled=True),
        lax.all_gather(masked_out, "fsdp", axis=1, tiled=True),
    )
    width = whole_rows.shape[1]
    own_width = tokens.shape[1]
    col_start = lax.axis_index("tp") * own_width
    gelu_exact = partial(jax.nn.gelu, approximate=False)
    values = whole_rows.astype(jnp.float32)
    centre = jnp.mean(values, axis=1, keepdims=True)
    centred = values - centre
    inv_std = lax.rsqrt(jnp.mean(centred * centred, axis=1, keepdims=True) + 1e-05)
    normed = centred * inv_std
    scaled = (normed * gain_full.astype(jnp.float32) + bias_full.astype(jnp.float32)).astype(
        jnp.bfloat16
    )
    hidden = jnp.dot(scaled, full_in, preferred_element_type=jnp.float32)
    active = gelu_exact(hidden).astype(jnp.bfloat16)
    partial_out = jnp.dot(active, full_out, preferred_element_type=jnp.float32)
    branch = lax.psum_scatter(
        partial_out.astype(jnp.bfloat16), "tp", scatter_dimension=1, tiled=True
    ).astype(jnp.float32)
    block_out = (tokens.astype(jnp.float32) + branch).astype(jnp.bfloat16)
    flags = frame_mask[:, None].astype(jnp.bfloat16)
    chosen = whole_grad * flags
    chosen_own = cotangent * flags
    back_active = contract_cols(chosen, full_out)
    unused, gelu_back = jax.vjp(gelu_exact, hidden)
    back_hidden = gelu_back(back_active)[0].astype(jnp.bfloat16)
    partial_normed = contract_cols(back_hidden, full_in)
    normed_own = lax.dynamic_slice_in_dim(normed, col_start, own_width, 1)
    gain_own = ln_gain.astype(jnp.float32)
    back_normed = lax.psum_scatter(
        partial_normed.astype(jnp.bfloat16), "tp", scatter_dimension=1, tiled=True
    ).astype(jnp.float32)
    back_scaled = back_normed * gain_own
    sum_plain = jnp.sum(back_scaled, axis=1)
    sum_cross = jnp.sum(back_scaled * normed_own, axis=1)
    sum_plain, sum_cross = lax.psum((sum_plain, sum_cross), "tp")
    mean_plain = (sum_plain / width)[:, None]
    mean_cross = (sum_cross / width)[:, None]
    back_rows = inv_std * (back_scaled - mean_plain - normed_own * mean_cross)
    input_grad = (chosen_own.astype(jnp.float32) + back_rows).astype(jnp.bfloat16)
    local_gain = jnp.sum(back_normed * normed_own, axis=0)
    local_bias = jnp.sum(back_normed, axis=0)
    grad_gain, grad_bias = lax.psum((local_gain, local_bias), ("rep", "fsdp"))
    term_in = contract_rows(scaled, back_hidden)
    term_out = contract_rows(active, chosen)
    shard_in, shard_out = (
        lax.psum_scatter(
            term_in.astype(jnp.bfloat16), "fsdp", scatter_dimension=0, tiled=True
        ).astype(jnp.float32),
        lax.psum_scatter(
            term_out.astype(jnp.bfloat16), "fsdp", scatter_dimension=1, tiled=True
        ).astype(jnp.float32),
    )
    shard_in, shard_out = (
        lax.psum(shard_in.astype(jnp.bfloat16), "rep").astype(jnp.float32),
        lax.psum(shard_out.astype(jnp.bfloat16), "rep").astype(jnp.float32),
    )
    grad_in = apply_blocks(shard_in, blocks_in, jnp.float32)
    grad_out = apply_blocks(shard_out, blocks_out, jnp.float32)
    return (block_out, input_grad, grad_in, grad_out, grad_gain, grad_bias)


def solution(mesh):
    placed = (
        P(("rep", "fsdp"), "tp"),
        P(("rep", "fsdp"), "tp"),
        P(("rep", "fsdp")),
        P("tp"),
        P("tp"),
        P("fsdp", "tp"),
        P("tp", "fsdp"),
        P("fsdp", "tp"),
        P("tp", "fsdp"),
    )
    return jax.shard_map(
        on_device,
        mesh=mesh,
        in_specs=placed,
        out_specs=(
            P(("rep", "fsdp"), "tp"),
            P(("rep", "fsdp"), "tp"),
            P("fsdp", "tp"),
            P("tp", "fsdp"),
            P("tp"),
            P("tp"),
        ),
        check_vma=False,
    )
```

profile of v0, /device:TPU:0, one launch (start us, length us, event | category | flops | bytes accessed | tf_op | source)
XLA Modules:
  0.0 492.1 jit_solution(3719068611543885792)
XLA Ops:
  9.2 2.4 bitcast_multiply_fusion.3
  12.0 1.2 bitcast_multiply_fusion.2
  13.8 22.1 %all-gather = bf16[16,1,128]{2,1,0:T(2,128)(2,1)S(1)} all-gather(bf16[1,1,128]{2,1,0:T(2,128)(2,1)S(1)} %bitcast.45), channel_id=1, replica_groups=mesh['rep'=4,'fsdp'=2,'tp'=16] {'tp'}, dimensions={0}, use_global_device_ids=true | all-gather | bytes 4352 | tf_op jit(solution)/shard_map/all_gather | solution.py:35
  36.0 19.5 %all-gather.1 = bf16[16,1,128]{2,1,0:T(2,128)(2,1)S(1)} all-gather(bf16[1,1,128]{2,1,0:T(2,128)(2,1)S(1)} %bitcast.44), channel_id=1, replica_groups=mesh['rep'=4,'fsdp'=2,'tp'=16] {'tp'}, dimensions={0}, use_global_device_ids=true | all-gather | bytes 4352 | tf_op jit(solution)/shard_map/all_gather | solution.py:36
  55.5 14.8 %all-gather.7.cloned.1.call-done = bf16[1024,2048]{1,0:T(8,128)(2,1)} async-done(((bf16[1024,128]{1,0:T(8,128)(2,1)}), bf16[1024,2048]{1,0:T(8,128)(2,1)}) %all-gather.7.cloned.1.call-update) | async-done | bytes 4194320 | tf_op jit(solution)/shard_map/all_gather | solution.py:33
  70.4 3.0 convert_reduce_fusion
  73.8 1.2 fusion.2
  75.1 10.1 %all-gather.9.cloned.1.call-done = bf16[2048,512]{1,0:T(8,128)(2,1)} async-done(((bf16[1024,512]{1,0:T(8,128)(2,1)}), bf16[2048,512]{1,0:T(8,128)(2,1)}) %all-gather.9.cloned.1.call-update) | async-done | bytes 2097168 | tf_op jit(solution)/shard_map/all_gather | solution.py:41
  85.1 10.5 %multiply_convert_fusion = (bf16[1024,512]{1,0:T(8,128)(2,1)S(1)}, f32[1024,512]{1,0:T(8,128)}, f32[1024,512]{1,0:T(8,128)}) fusion(bf16[2048,512]{1,0:T(8,128)(2,1)} %all-gather.9.cloned.1.call-done, f32[2048]{0:T(1024)S(1)} %bitcast.42, f32[2048]{0:T(1024)S(1)} %bitcast.40, f32[1024]{0:T(1024)S(1)} %add_rsqrt_fusion, ...), kind=kOutput, calls=%fused_computation.21 | convolution fusion | flops 2194145280 | bytes 11558912 | tf_op jit(solution)/shard_map/dot_general | solution.py:56
  95.6 5.8 %all-gather.11.cloned.1.call-done = bf16[512,2048]{1,0:T(8,128)(2,1)} async-done(((bf16[512,1024]{1,0:T(8,128)(2,1)}), bf16[512,2048]{1,0:T(8,128)(2,1)}) %all-gather.11.cloned.1.call-update) | async-done | bytes 2097168 | tf_op jit(solution)/shard_map/all_gather | solution.py:42
  101.4 61.1 %all-gather.13.cloned.1.call-done = bf16[1024,2048]{1,0:T(8,128)(2,1)} async-done(((bf16[1024,128]{1,0:T(8,128)(2,1)}), bf16[1024,2048]{1,0:T(8,128)(2,1)}) %all-gather.13.cloned.1.call-update) | async-done | bytes 4194320 | tf_op jit(solution)/shard_map/all_gather | solution.py:34
  162.5 7.1 %add_convert_fusion.1 = bf16[1024,512]{1,0:T(8,128)(2,1)S(1)} fusion(f32[1024,512]{1,0:T(8,128)} %get-tuple-element.17, f32[1024,512]{1,0:T(8,128)} %get-tuple-element.22, bf16[512,2048]{1,0:T(8,128)(2,1)} %all-gather.11.cloned.1.call-done, bf16[1024,2048]{1,0:T(8,128)(2,1)} %all-gather.13.cloned.1.call-done, bf16[1024]{0:T(1024)(128)(2,1)S(1)} %convert_element_type.88), kind=kOutput, calls=%fused_computation.18 | convolution fusion | flops 2156920832 | bytes 11536384 | tf_op jit(solution)/shard_map/dot_general | solution.py:24
  170.7 4.4 convolution_convert_fusion.2
  175.4 6.0 %fusion.7 = bf16[512,2048]{1,0:T(8,128)(2,1)} fusion(bf16[1024,512]{1,0:T(8,128)(2,1)S(1)} %get-tuple-element.16, bf16[1024,2048]{1,0:T(8,128)(2,1)} %all-gather.13.cloned.1.call-done, bf16[1024]{0:T(1024)(128)(2,1)S(1)} %convert_element_type.88), kind=kOutput, calls=%fused_computation.14 | convolution fusion | flops 2150629376 | bytes 7342080 | tf_op jit(solution)/shard_map/dot_general | solution.py:18
  181.4 5.3 %reduce-scatter.9.cloned.1.call-done = bf16[1024,512]{1,0:T(8,128)(2,1)} async-done(((bf16[2048,512]{1,0:T(8,128)(2,1)}), bf16[1024,512]{1,0:T(8,128)(2,1)}) %reduce-scatter.9.cloned.1.call-update) | async-done | bytes 1048592 | tf_op jit(solution)/shard_map/reduce_scatter | solution.py:89
  186.7 16.6 %reduce-scatter.11.cloned.1.call-done = bf16[512,1024]{1,0:T(8,128)(2,1)} async-done(((bf16[512,2048]{1,0:T(8,128)(2,1)}), bf16[512,1024]{1,0:T(8,128)(2,1)}) %reduce-scatter.11.cloned.1.call-update) | async-done | bytes 1048592 | tf_op jit(solution)/shard_map/reduce_scatter | solution.py:92
  203.4 5.5 %convolution_convert_fusion = bf16[1024,2048]{1,0:T(8,128)(2,1)} fusion(bf16[1024,512]{1,0:T(8,128)(2,1)} %copy-done.14, bf16[2048,512]{1,0:T(8,128)(2,1)S(1)} %copy-done.11), kind=kOutput, calls=%fused_computation.6 | convolution fusion | flops 2149580800 | bytes 7340032 | tf_op jit(solution)/shard_map/dot_general | solution.py:24
  208.9 6.4 %copy.21 = bf16[1024,2048]{0,1:T(8,128)(2,1)} copy(bf16[1024,2048]{1,0:T(8,128)(2,1)} %convolution_convert_fusion) | data formatting | bytes 8388608
  215.4 1.6 copy-done.12
  217.0 5.5 %convolution_convert_fusion.1 = bf16[1024,2048]{1,0:T(8,128)(2,1)} fusion(bf16[1024,512]{1,0:T(8,128)(2,1)} %copy-done.13, bf16[512,2048]{1,0:T(8,128)(2,1)S(1)} %copy-done.12), kind=kOutput, calls=%fused_computation.7 | convolution fusion | flops 2149580800 | bytes 7340032 | tf_op jit(solution)/shard_map/dot_general | solution.py:58
  222.5 6.4 %copy.19 = bf16[1024,2048]{0,1:T(8,128)(2,1)} copy(bf16[1024,2048]{1,0:T(8,128)(2,1)} %convolution_convert_fusion.1) | data formatting | bytes 8388608
  229.0 6.4 %fusion = f32[1024,2048]{1,0:T(8,128)} fusion(bf16[1024,2048]{1,0:T(8,128)(2,1)} %all-gather.7.cloned.1.call-done, f32[1024]{0:T(1024)S(1)} %add_rsqrt_fusion, f32[1024]{0:T(1024)S(1)} %broadcast_multiply_fusion.2), kind=kLoop, calls=%fused_computation.2 | loop fusion | flops 6291456 | bytes 12591104 | tf_op jit(solution)/shard_map/mul | solution.py:52
  235.4 30.6 %all-reduce.5.cloned.1.call-done = (bf16[1024,512]{1,0:T(8,128)(2,1)}, bf16[512,1024]{1,0:T(8,128)(2,1)}) async-done(((bf16[1024,512]{1,0:T(8,128)(2,1)}, bf16[512,1024]{1,0:T(8,128)(2,1)}), (bf16[1024,512]{1,0:T(8,128)(2,1)}, bf16[512,1024]{1,0:T(8,128)(2,1)})) %all-reduce.5.cloned.1.call-update) | async-done | bytes 2097168 | tf_op jit(solution)/shard_map/psum | solution.py:97
  267.3 1.7 bitcast_multiply_fusion.1
  270.2 2.0 bitcast_multiply_fusion
  272.2 75.3 %reduce-scatter.15.cloned.1.call-done = bf16[128,1024]{1,0:T(8,128)(2,1)} async-done(((bf16[2048,1024]{1,0:T(8,128)(2,1)}), bf16[128,1024]{1,0:T(8,128)(2,1)}) %reduce-scatter.15.cloned.1.call-update) | async-done | bytes 262160
  348.5 79.2 %reduce-scatter.13.cloned.1.call-done = bf16[128,1024]{1,0:T(8,128)(2,1)} async-done(((bf16[2048,1024]{1,0:T(8,128)(2,1)}), bf16[128,1024]{1,0:T(8,128)(2,1)}) %reduce-scatter.13.cloned.1.call-update) | async-done | bytes 262160
  427.7 1.1 copy.20
  429.6 1.4 fusion.29
  431.0 13.5 %all-reduce.1 = (f32[128]{0:T(128)}, f32[128]{0:T(128)}) all-reduce(f32[128]{0:T(128)S(1)} %get-tuple-element.6, f32[128]{0:T(128)S(1)} %get-tuple-element.9), channel_id=1, replica_groups=mesh['rep'=4,'fsdp'=2,'tp'=16] {'rep','fsdp'}, use_global_device_ids=true, to_apply=%region_13.0 | all-reduce | flops 256 | bytes 2048 | tf_op jit(solution)/shard_map/psum | solution.py:85
  444.5 38.7 %all-reduce = (f32[1024]{0:T(1024)S(1)}, f32[1024]{0:T(1024)S(1)}) all-reduce(f32[1024]{0:T(1024)S(1)} %get-tuple-element.7, f32[1024]{0:T(1024)S(1)} %get-tuple-element.8), channel_id=1, replica_groups=mesh['rep'=4,'fsdp'=2,'tp'=16] {'tp'}, use_global_device_ids=true, to_apply=%region_7.0 | all-reduce | flops 2048 | bytes 16384 | tf_op jit(solution)/shard_map/psum | solution.py:78
  483.2 2.4 fusion.27
  (64 shorter events, 9.2 us)
Async XLA Ops:
  7.2 63.2 %all-gather.7.cloned.1.call-start = ((), (), s32[]{:S(2)}) async-start(), calls=%async_computation.4 | async-start | bytes 4456448 | tf_op jit(solution)/shard_map/all_gather | solution.py:33
  7.9 77.2 %all-gather.9.cloned.1.call-start = ((), (), s32[]{:S(2)}) async-start(), calls=%async_computation.5 | async-start | bytes 3145728 | tf_op jit(solution)/shard_map/all_gather | solution.py:41
  9.2 2.5 copy-start.8
  9.2 2.7 copy-start.2
  11.6 89.8 %all-gather.11.cloned.1.call-start = ((), (), s32[]{:S(2)}) async-start(), calls=%async_computation.6 | async-start | bytes 3145728 | tf_op jit(solution)/shard_map/all_gather | solution.py:42
  11.9 1.9 copy-start.10
  11.9 24.1 %copy-start.9 = (bf16[128]{0:T(256)(128)(2,1)S(1)}, bf16[128]{0:T(256)(128)(2,1)}, u32[]{:S(2)}) copy-start(bf16[128]{0:T(256)(128)(2,1)} %param.13) | copy-start | bytes 772
  11.9 43.6 %copy-start.7 = (s32[1024]{0:T(1024)S(1)}, s32[1024]{0:T(1024)}, u32[]{:S(2)}) copy-start(s32[1024]{0:T(1024)} %param.11) | copy-start | bytes 12292
  13.2 149.3 %all-gather.13.cloned.1.call-start = ((), (), s32[]{:S(2)}) async-start(), calls=%async_computation.7 | async-start | bytes 4456448 | tf_op jit(solution)/shard_map/all_gather | solution.py:34
  13.8 173.0 %reduce-scatter.9.cloned.1.call-start = ((), (), s32[]{:S(2)}) async-start(), calls=%async_computation.8 | async-start | bytes 3145728 | tf_op jit(solution)/shard_map/reduce_scatter | solution.py:89
  70.4 3.4 copy-start
  95.6 79.8 %copy-start.13 = (bf16[1024,512]{1,0:T(8,128)(2,1)}, bf16[1024,512]{1,0:T(8,128)(2,1)S(1)}, u32[]{:S(2)}) copy-start(bf16[1024,512]{1,0:T(8,128)(2,1)S(1)} %get-tuple-element.16) | copy-start | bytes 3145732
  162.5 8.1 %copy-start.1 = (bf16[1024,2048]{1,0:T(8,128)(2,1)S(1)}, bf16[1024,2048]{1,0:T(8,128)(2,1)}, u32[]{:S(2)}) copy-start(bf16[1024,2048]{1,0:T(8,128)(2,1)} %all-gather.7.cloned.1.call-done) | copy-start | bytes 12582916
  169.6 1.0 copy-start.14
  175.1 28.2 %reduce-scatter.11.cloned.1.call-start = ((), (), s32[]{:S(2)}) async-start(), calls=%async_computation.9 | async-start | bytes 3145728 | tf_op jit(solution)/shard_map/reduce_scatter | solution.py:92
  181.3 22.1 %copy-start.11 = (bf16[2048,512]{1,0:T(8,128)(2,1)S(1)}, bf16[2048,512]{1,0:T(8,128)(2,1)}, u32[]{:S(2)}) copy-start(bf16[2048,512]{1,0:T(8,128)(2,1)} %all-gather.9.cloned.1.call-done) | copy-start | bytes 6291460
  181.4 84.7 %all-reduce.5.cloned.1.call-start = ((), (), s32[]{:S(2)}) async-start(), calls=%async_computation.12 | async-start | bytes 4194304 | tf_op jit(solution)/shard_map/psum | solution.py:97
  203.3 144.1 %reduce-scatter.15.cloned.1.call-start = ((), (), s32[]{:S(2)}) async-start(), calls=%async_computation.11 | async-start | bytes 4456448
  215.3 1.6 copy-start.12
  215.3 212.4 %reduce-scatter.13.cloned.1.call-start = ((), (), s32[]{:S(2)}) async-start(), calls=%async_computation.10 | async-start | bytes 4456448
  266.0 1.2 copy-start.4
  268.9 1.2 copy-start.3
  270.2 158.7 %copy-start.5 = (bf16[1024,128]{1,0:T(8,128)(2,1)S(1)}, bf16[1024,128]{1,0:T(8,128)(2,1)}, u32[]{:S(2)}) copy-start(bf16[1024,128]{1,0:T(8,128)(2,1)} %param.9) | copy-start | bytes 786436
  272.2 211.0 %copy-start.6 = (bf16[1024,128]{1,0:T(8,128)(2,1)S(1)}, bf16[1024,128]{1,0:T(8,128)(2,1)}, u32[]{:S(2)}) copy-start(bf16[1024,128]{1,0:T(8,128)(2,1)} %param.10) | copy-start | bytes 786436
Sparse Core Ops, SparseCore 0:
  10.1 60.2 all-gather.6
  72.6 12.4 all-gather.8
  86.8 14.6 all-gather.10
  103.4 59.0 all-gather.12
  175.2 11.4 reduce-scatter.8
  189.6 13.6 reduce-scatter.10
  205.8 60.2 all-reduce.4
  269.7 77.6 reduce-scatter.14
  350.8 76.9 reduce-scatter.12
where the time goes:
time: 493 us; the launch traced here: 492 us
  waiting for transfers between devices  300 us (61%)
  blocking collectives  93.8 us (19%)
  matrix products  39 us (8%)
  other arithmetic  23.2 us (5%)
  local copies, waits for them, and re-layouts  21.3 us (4%)
  between operations  14.1 us (3%)
    unnamed x11, waiting for transfers between devices  156 us
    all_gather x1, waiting for transfers between devices, on_device(): lax.all_gather(cotangent, 'tp', axis=1, tiled=True)  61.1 us
    psum x1, blocking collectives, on_device(): sum_plain, sum_cross = lax.psum((sum_plain, sum_cross), 'tp')  38.7 us
    psum x1, waiting for transfers between devices, on_device(): lax.psum(shard_in.astype(jnp.bfloat16), 'rep').astype(jnp.float32)  30.6 us
    all_gather x1, blocking collectives, on_device(): lax.all_gather(ln_gain, 'tp', axis=0, tiled=True)  22.1 us
    unnamed x34, local copies, waits for them, and re-layouts  20 us
    all_gather x1, blocking collectives, on_device(): lax.all_gather(ln_bias, 'tp', axis=0, tiled=True)  19.5 us
    reduce_scatter x1, waiting for transfers between devices, on_device(): lax.psum_scatter(term_out.astype(jnp.bfloat16), 'fsdp', scatter_dimension...  16.6 us
  transfers between devices with their start and end apart: 9, of which 9 were waited for; matrix products, arithmetic and copies ran while one was open for 12% of the time, Pallas kernels for 0%

commit v1 on v0

--- a/solution.py
+++ b/solution.py
@@ -38,7 +38,9 @@
     masked_in = apply_blocks(weight_in, blocks_in, jnp.bfloat16)
     masked_out = apply_blocks(weight_out, blocks_out, jnp.bfloat16)
     full_in, full_out = (
-        lax.all_gather(masked_in, "fsdp", axis=0, tiled=True),
+        jnp.concatenate(
+            lax.all_to_all(jnp.stack([masked_in] * lax.axis_size("fsdp")), "fsdp", 0, 0), axis=0
+        ),
         lax.all_gather(masked_out, "fsdp", axis=1, tiled=True),
     )
     width = whole_rows.shape[1]

time: 493 us -> 476 us (0.966)
  waiting for transfers between devices: 300 us -> 280 us
    all_gather x1 -> x0, waiting for transfers between devices: 10.1 us -> none  [on_device(): lax.all_gather(masked_in, 'fsdp', axis=0, tiled=True)]
    all_gather x1, waiting for transfers between devices: 5.84 us -> 0.01 us  [on_device(): lax.all_gather(masked_out, 'fsdp', axis=1, tiled=True)]
    unnamed x11 -> x10, waiting for transfers between devices: 156 us -> 155 us
    unnamed x34 -> x30, local copies, waits for them, and re-layouts: 20 us -> 19.6 us
  transfers between devices with their start and end apart: 9 -> 9, of which waited for: 9 -> 7; matrix products, arithmetic and copies ran while one was open for 12% -> 13% of each run, Pallas kernels for 0% -> 0%
where the time goes in v1:
time: 476 us; the launch traced here: 474 us
  waiting for transfers between devices  280 us (59%)
  blocking collectives  93.2 us (20%)
  matrix products  37.6 us (8%)
  other arithmetic  23.7 us (5%)
  local copies, waits for them, and re-layouts  20.8 us (4%)
  between operations  14.4 us (3%)
    unnamed x10, waiting for transfers between devices  155 us
    all_gather x1, waiting for transfers between devices, on_device(): lax.all_gather(cotangent, 'tp', axis=1, tiled=True)  60.9 us
    psum x1, blocking collectives, on_device(): sum_plain, sum_cross = lax.psum((sum_plain, sum_cross), 'tp')  38.7 us
    psum x1, waiting for transfers between devices, on_device(): lax.psum(shard_in.astype(jnp.bfloat16), 'rep').astype(jnp.float32)  31.8 us
    all_gather x1, blocking collectives, on_device(): lax.all_gather(ln_bias, 'tp', axis=0, tiled=True)  22.2 us
    unnamed x30, local copies, waits for them, and re-layouts  19.6 us
    all_gather x1, blocking collectives, on_device(): lax.all_gather(ln_gain, 'tp', axis=0, tiled=True)  19.5 us
    reduce_scatter x1, waiting for transfers between devices, on_device(): lax.psum_scatter(term_out.astype(jnp.bfloat16), 'fsdp', scatter_dimension...  16.6 us
  transfers between devices with their start and end apart: 9, of which 7 were waited for; matrix products, arithmetic and copies ran while one was open for 13% of the time, Pallas kernels for 0%

profile of v1, /device:TPU:0, one launch (start us, length us, event | category | flops | bytes accessed | tf_op | source)
XLA Modules:
  0.0 474.2 jit_solution(7285723251199019257)
XLA Ops:
  8.9 2.4 bitcast_multiply_fusion.2
  12.8 1.5 pad_maximum_fusion
  14.3 3.9 all-to-all-start
  18.3 22.2 %all-gather.1 = bf16[16,1,128]{2,1,0:T(2,128)(2,1)S(1)} all-gather(bf16[1,1,128]{2,1,0:T(2,128)(2,1)S(1)} %bitcast.51), channel_id=1, replica_groups=mesh['rep'=4,'fsdp'=2,'tp'=16] {'tp'}, dimensions={0}, use_global_device_ids=true | all-gather | bytes 4352 | tf_op jit(solution)/shard_map/all_gather | solution.py:36
  40.4 19.5 %all-gather = bf16[16,1,128]{2,1,0:T(2,128)(2,1)S(1)} all-gather(bf16[1,1,128]{2,1,0:T(2,128)(2,1)S(1)} %bitcast.52), channel_id=1, replica_groups=mesh['rep'=4,'fsdp'=2,'tp'=16] {'tp'}, dimensions={0}, use_global_device_ids=true | all-gather | bytes 4352 | tf_op jit(solution)/shard_map/all_gather | solution.py:35
  60.0 10.4 %all-gather.6.cloned.1.call-done = bf16[1024,2048]{1,0:T(8,128)(2,1)} async-done(((bf16[1024,128]{1,0:T(8,128)(2,1)}), bf16[1024,2048]{1,0:T(8,128)(2,1)}) %all-gather.6.cloned.1.call-update) | async-done | bytes 4194320 | tf_op jit(solution)/shard_map/all_gather | solution.py:33
  70.4 3.0 convert_reduce_fusion
  73.8 1.2 fusion.2
  75.1 9.8 %multiply_convert_fusion = (bf16[1024,512]{1,0:T(8,128)(2,1)S(1)}, f32[1024,512]{1,0:T(8,128)}, f32[1024,512]{1,0:T(8,128)}) fusion(bf16[2048,512]{1,0:T(8,128)(2,1)S(1)} %bitcast.43, f32[2048]{0:T(1024)S(1)} %bitcast.47, f32[2048]{0:T(1024)S(1)} %bitcast.49, f32[1024]{0:T(1024)S(1)} %add_rsqrt_fusion, f32[1024]{0:T(1024)S(1)} %broadcast_multiply_fusion.2, ...), kind=kOutput, calls=%fused_computation.22 | convolution fusion | flops 2194145280 | bytes 11558912 | tf_op jit(solution)/shard_map/dot_general | solution.py:58
  84.9 60.9 %all-gather.10.cloned.1.call-done = bf16[1024,2048]{1,0:T(8,128)(2,1)} async-done(((bf16[1024,128]{1,0:T(8,128)(2,1)}), bf16[1024,2048]{1,0:T(8,128)(2,1)}) %all-gather.10.cloned.1.call-update) | async-done | bytes 4194320 | tf_op jit(solution)/shard_map/all_gather | solution.py:34
  145.8 7.1 %add_convert_fusion.1 = bf16[1024,512]{1,0:T(8,128)(2,1)S(1)} fusion(f32[1024,512]{1,0:T(8,128)} %get-tuple-element.17, f32[1024,512]{1,0:T(8,128)} %get-tuple-element.22, bf16[512,2048]{1,0:T(8,128)(2,1)} %all-gather.8.cloned.1.call-done, bf16[1024,2048]{1,0:T(8,128)(2,1)} %all-gather.10.cloned.1.call-done, bf16[1024]{0:T(1024)(128)(2,1)S(1)} %convert_element_type.88), kind=kOutput, calls=%fused_computation.19 | convolution fusion | flops 2156920832 | bytes 11536384 | tf_op jit(solution)/shard_map/dot_general | solution.py:24
  153.9 4.5 convolution_convert_fusion.2
  158.6 6.0 %fusion.7 = bf16[512,2048]{1,0:T(8,128)(2,1)} fusion(bf16[1024,512]{1,0:T(8,128)(2,1)S(1)} %get-tuple-element.16, bf16[1024,2048]{1,0:T(8,128)(2,1)} %all-gather.10.cloned.1.call-done, bf16[1024]{0:T(1024)(128)(2,1)S(1)} %convert_element_type.88), kind=kOutput, calls=%fused_computation.14 | convolution fusion | flops 2150629376 | bytes 7342080 | tf_op jit(solution)/shard_map/dot_general | solution.py:18
  164.7 5.3 %reduce-scatter.9.cloned.1.call-done = bf16[1024,512]{1,0:T(8,128)(2,1)} async-done(((bf16[2048,512]{1,0:T(8,128)(2,1)}), bf16[1024,512]{1,0:T(8,128)(2,1)}) %reduce-scatter.9.cloned.1.call-update) | async-done | bytes 1048592 | tf_op jit(solution)/shard_map/reduce_scatter | solution.py:91
  170.0 16.6 %reduce-scatter.11.cloned.1.call-done = bf16[512,1024]{1,0:T(8,128)(2,1)} async-done(((bf16[512,2048]{1,0:T(8,128)(2,1)}), bf16[512,1024]{1,0:T(8,128)(2,1)}) %reduce-scatter.11.cloned.1.call-update) | async-done | bytes 1048592 | tf_op jit(solution)/shard_map/reduce_scatter | solution.py:94
  186.6 5.9 %convolution_convert_fusion.1 = bf16[1024,2048]{1,0:T(8,128)(2,1)} fusion(bf16[1024,512]{1,0:T(8,128)(2,1)S(1)} %get-tuple-element.16, bf16[512,2048]{1,0:T(8,128)(2,1)} %all-gather.8.cloned.1.call-done), kind=kOutput, calls=%fused_computation.7 | convolution fusion | flops 2149580800 | bytes 7340032 | tf_op jit(solution)/shard_map/dot_general | solution.py:60
  192.5 6.4 %copy.19 = bf16[1024,2048]{0,1:T(8,128)(2,1)} copy(bf16[1024,2048]{1,0:T(8,128)(2,1)} %convolution_convert_fusion.1) | data formatting | bytes 8388608
  198.9 1.2 copy-done.12
  200.1 4.3 convolution_convert_fusion
  204.4 6.4 %copy.21 = bf16[1024,2048]{0,1:T(8,128)(2,1)} copy(bf16[1024,2048]{1,0:T(8,128)(2,1)} %convolution_convert_fusion) | data formatting | bytes 8388608
  211.0 6.4 %fusion = f32[1024,2048]{1,0:T(8,128)} fusion(bf16[1024,2048]{1,0:T(8,128)(2,1)} %all-gather.6.cloned.1.call-done, f32[1024]{0:T(1024)S(1)} %add_rsqrt_fusion, f32[1024]{0:T(1024)S(1)} %broadcast_multiply_fusion.2), kind=kLoop, calls=%fused_computation.2 | loop fusion | flops 6291456 | bytes 12591104 | tf_op jit(solution)/shard_map/mul | solution.py:54
  217.4 31.8 %all-reduce.5.cloned.1.call-done = (bf16[1024,512]{1,0:T(8,128)(2,1)}, bf16[512,1024]{1,0:T(8,128)(2,1)}) async-done(((bf16[1024,512]{1,0:T(8,128)(2,1)}, bf16[512,1024]{1,0:T(8,128)(2,1)}), (bf16[1024,512]{1,0:T(8,128)(2,1)}, bf16[512,1024]{1,0:T(8,128)(2,1)})) %all-reduce.5.cloned.1.call-update) | async-done | bytes 2097168 | tf_op jit(solution)/shard_map/psum | solution.py:99
  250.4 1.7 bitcast_multiply_fusion.1
  253.3 2.0 bitcast_multiply_fusion
  255.3 75.3 %reduce-scatter.13.cloned.1.call-done = bf16[128,1024]{1,0:T(8,128)(2,1)} async-done(((bf16[2048,1024]{1,0:T(8,128)(2,1)}), bf16[128,1024]{1,0:T(8,128)(2,1)}) %reduce-scatter.13.cloned.1.call-update) | async-done | bytes 262160
  330.5 1.1 copy.20
  332.4 78.4 %reduce-scatter.15.cloned.1.call-done = bf16[128,1024]{1,0:T(8,128)(2,1)} async-done(((bf16[2048,1024]{1,0:T(8,128)(2,1)}), bf16[128,1024]{1,0:T(8,128)(2,1)}) %reduce-scatter.15.cloned.1.call-update) | async-done | bytes 262160
  410.8 1.1 copy.22
  411.9 1.4 fusion.30
  413.3 38.7 %all-reduce = (f32[1024]{0:T(1024)S(1)}, f32[1024]{0:T(1024)S(1)}) all-reduce(f32[1024]{0:T(1024)S(1)} %get-tuple-element.7, f32[1024]{0:T(1024)S(1)} %get-tuple-element.8), channel_id=1, replica_groups=mesh['rep'=4,'fsdp'=2,'tp'=16] {'tp'}, use_global_device_ids=true, to_apply=%region_7.0 | all-reduce | flops 2048 | bytes 16384 | tf_op jit(solution)/shard_map/psum | solution.py:80
  452.1 2.4 fusion.28
  454.4 12.9 %all-reduce.1 = (f32[128]{0:T(128)}, f32[128]{0:T(128)}) all-reduce(f32[128]{0:T(128)S(1)} %get-tuple-element.6, f32[128]{0:T(128)S(1)} %get-tuple-element.9), channel_id=1, replica_groups=mesh['rep'=4,'fsdp'=2,'tp'=16] {'rep','fsdp'}, use_global_device_ids=true, to_apply=%region_13.0 | all-reduce | flops 256 | bytes 2048 | tf_op jit(solution)/shard_map/psum | solution.py:87
  (60 shorter events, 8.4 us)
Async XLA Ops:
  7.2 63.2 %all-gather.6.cloned.1.call-start = ((), (), s32[]{:S(2)}) async-start(), calls=%async_computation.5 | async-start | bytes 4456448 | tf_op jit(solution)/shard_map/all_gather | solution.py:33
  7.9 77.0 %all-gather.8.cloned.1.call-start = ((), (), s32[]{:S(2)}) async-start(), calls=%async_computation.6 | async-start | bytes 3145728 | tf_op jit(solution)/shard_map/all_gather | solution.py:44
  8.9 3.2 copy-start.8
  8.9 3.7 copy-start.2
  11.4 134.4 %all-gather.10.cloned.1.call-start = ((), (), s32[]{:S(2)}) async-start(), calls=%async_computation.7 | async-start | bytes 4456448 | tf_op jit(solution)/shard_map/all_gather | solution.py:34
  14.3 4.0 copy-start.9
  14.3 26.1 %copy-start.10 = (bf16[128]{0:T(256)(128)(2,1)S(1)}, bf16[128]{0:T(256)(128)(2,1)}, u32[]{:S(2)}) copy-start(bf16[128]{0:T(256)(128)(2,1)} %param.12) | copy-start | bytes 772
  14.3 45.7 %copy-start.7 = (s32[1024]{0:T(1024)S(1)}, s32[1024]{0:T(1024)}, u32[]{:S(2)}) copy-start(s32[1024]{0:T(1024)} %param.11) | copy-start | bytes 12292
  14.3 60.8 %all-to-all-start = ((bf16[2,1024,512]{2,1,0:T(8,128)(2,1)}), bf16[2,1024,512]{2,1,0:T(8,128)(2,1)S(1)}, u32[]{:S(2)}, u32[]{:S(2)}) async-start(bf16[2,1024,512]{2,1,0:T(8,128)(2,1)} %pad_maximum_fusion), calls=%async_computation | async-start | bytes 4194304 | tf_op jit(solution)/shard_map/all_to_all | solution.py:42
  18.2 151.8 %reduce-scatter.9.cloned.1.call-start = ((), (), s32[]{:S(2)}) async-start(), calls=%async_computation.8 | async-start | bytes 3145728 | tf_op jit(solution)/shard_map/reduce_scatter | solution.py:91
  70.4 3.4 copy-start
  145.8 8.1 %copy-start.1 = (bf16[1024,2048]{1,0:T(8,128)(2,1)S(1)}, bf16[1024,2048]{1,0:T(8,128)(2,1)}, u32[]{:S(2)}) copy-start(bf16[1024,2048]{1,0:T(8,128)(2,1)} %all-gather.6.cloned.1.call-done) | copy-start | bytes 12582916
  152.9 1.0 copy-start.11
  158.4 28.2 %reduce-scatter.11.cloned.1.call-start = ((), (), s32[]{:S(2)}) async-start(), calls=%async_computation.9 | async-start | bytes 3145728 | tf_op jit(solution)/shard_map/reduce_scatter | solution.py:94
  164.6 84.5 %all-reduce.5.cloned.1.call-start = ((), (), s32[]{:S(2)}) async-start(), calls=%async_computation.12 | async-start | bytes 4194304 | tf_op jit(solution)/shard_map/psum | solution.py:99
  186.6 143.9 %reduce-scatter.13.cloned.1.call-start = ((), (), s32[]{:S(2)}) async-start(), calls=%async_computation.10 | async-start | bytes 4456448
  198.9 1.2 copy-start.12
  198.9 211.9 %reduce-scatter.15.cloned.1.call-start = ((), (), s32[]{:S(2)}) async-start(), calls=%async_computation.11 | async-start | bytes 4456448
  249.1 1.2 copy-start.4
  252.1 1.2 copy-start.3
  253.3 78.4 %copy-start.5 = (bf16[1024,128]{1,0:T(8,128)(2,1)S(1)}, bf16[1024,128]{1,0:T(8,128)(2,1)}, u32[]{:S(2)}) copy-start(bf16[1024,128]{1,0:T(8,128)(2,1)} %param.9) | copy-start | bytes 786436
  255.3 196.8 %copy-start.6 = (bf16[1024,128]{1,0:T(8,128)(2,1)S(1)}, bf16[1024,128]{1,0:T(8,128)(2,1)}, u32[]{:S(2)}) copy-start(bf16[1024,128]{1,0:T(8,128)(2,1)} %param.10) | copy-start | bytes 786436
Sparse Core Ops, SparseCore 0:
  10.1 60.2 all-gather.5
  72.0 12.4 all-gather.7
  86.7 59.0 all-gather.9
  158.5 11.4 reduce-scatter.8
  172.9 13.6 reduce-scatter.10
  188.9 60.2 all-reduce.4
  252.8 77.6 reduce-scatter.12
  333.9 76.9 reduce-scatter.14
